TPU v7x, 128 devices: a whole 4x4x4 slice. The times are simulated.
128 devices in a mesh: rep: 4 (over x), shard: 32 (over z, y, core).
Axes of the slice: x: 4, y: 4, z: 4, core: 2. Of those that a mesh axis runs over, the one named last changes fastest.
Arguments:
- features: bfloat16 [65536, 1024], P(('rep', 'shard')), may hold values from -6 to 6
- cotangent: bfloat16 [65536, 1024], P(('rep', 'shard')), may hold values from -6 to 6
- cross_weight: bfloat16 [1024, 1024], replicated, may hold values from -0.1875 to 0.1875
- cross_bias: float32 [1024], replicated, may hold values from -3 to 3
- emb_table: float32 [131072, 128], P('shard'), may hold values from -6 to 6
- row_accum: float32 [131072], P('shard'), may hold values from 0.5 to 50
- send_bags: int32 [128, 32, 256], P(('rep', 'shard')), may hold values from 0 to 3583, as said below
- slot_counts: int32 [128, 32], P(('rep', 'shard')), may hold values from 64 to 256, as said below
- recv_rows: int32 [128, 32, 256], P(('rep', 'shard')), may hold values from 0 to 4095, as said below
- touched_rows: int32 [32, 2048], P('shard'), may hold values from 0 to 4095, as said below
Outputs:
- weight_grad: float32 [1024, 1024], replicated
- bias_grad: float32 [1024], replicated
- dense_grad: bfloat16 [65536, 128], P(('rep', 'shard'))
- new_table: float32 [131072, 128], P('shard')
- new_accum: float32 [131072], P('shard')
Inputs may be any that keep to these rules, and one draw needn't show every extreme that they name: `send_bags`: bag b * 7 + f of a device is feature f of its sample b. The first slot_counts[d, s] slots of a block are live; in each replica group some shard receives 256 live slots from every device of the group. `recv_rows`: every slot, live or not, names a row listed in touched_rows for the owner's shard. `touched_rows`: ascending and distinct.
All inputs are finite; a program needn't handle non-finite values.
Results may differ from a plain program's by a relative error of at most 0.0055.
Values may be sent and summed in bfloat16 or wider, within the bound.
No kernel may reach another device: no remote copies, remote signals or barrier semaphores. Data moves between devices by JAX's collectives and lax.ppermute only.
A program may use at most 128 MiB of HBM per device.

v0:
```python
import math
import jax
import jax.numpy as jnp
from jax import lax
from jax.sharding import PartitionSpec as P

learn_rate = 0.5
keep_rate = 0.9


def adagrad_rows(table_rows, accum_rows, grads):
    new_accum = accum_rows + jnp.mean(grads * grads, axis=1)
    new_rows = keep_rate * table_rows - learn_rate * grads / jnp.sqrt(new_accum)[:, None]
    return (new_rows, new_accum)


def blocked(count, fn):
    step_rows = math.gcd(count, 512)
    index_blocks = jnp.arange(count, dtype=jnp.int32).reshape(-1, step_rows)
    result = lax.map(fn, index_blocks)
    return result.reshape((count,) + result.shape[2:])


def per_device(
    features,
    cotangent,
    cross_weight,
    cross_bias,
    emb_table,
    row_accum,
    send_bags,
    slot_counts,
    recv_rows,
    touched_rows,
):
    width = emb_table.shape[1]
    shard_rows = emb_table.shape[0]
    total_tokens = features.shape[0] * lax.axis_size("rep") * lax.axis_size("shard")
    scale = 1.0 / jnp.sqrt(jnp.float32(total_tokens))
    linear = jnp.dot(features, cross_weight, preferred_element_type=jnp.float32) + cross_bias
    cot_f = cotangent.astype(jnp.float32)
    gated = (cot_f * features.astype(jnp.float32)).astype(jnp.bfloat16)
    weight_part = lax.dot_general(
        features, gated, (((0,), (0,)), ((), ())), preferred_element_type=jnp.float32
    )
    bias_part = jnp.sum(gated.astype(jnp.float32), axis=0)
    backprop = lax.dot_general(
        gated, cross_weight, (((1,), (1,)), ((), ())), preferred_element_type=jnp.float32
    )
    input_grad = cot_f * linear + backprop + cot_f
    dense_grad = input_grad[:, :width].astype(jnp.bfloat16)
    pooled = input_grad[:, width:].astype(jnp.bfloat16).reshape(-1, width)
    bag_ids = send_bags[0]
    shard_count = bag_ids.shape[0]
    slot_total = bag_ids.shape[1]
    live_mask = jnp.arange(slot_total, dtype=jnp.int32)[None, :] < slot_counts[0][:, None]
    flat_bags = jnp.where(live_mask, bag_ids, -1).reshape(-1)
    bag_range = jnp.arange(pooled.shape[0], dtype=jnp.int32)

    def pick_bags(positions):
        select = (flat_bags[positions][:, None] == bag_range[None, :]).astype(jnp.bfloat16)
        return jnp.dot(select, pooled, preferred_element_type=jnp.float32).astype(jnp.bfloat16)

    outgoing = blocked(shard_count * slot_total, pick_bags).reshape(shard_count, slot_total, width)
    incoming = lax.all_to_all(outgoing, "shard", split_axis=0, concat_axis=0, tiled=True)
    weight_sum, bias_sum = lax.psum((weight_part, bias_part), ("rep", "shard"))
    weight_grad = weight_sum * scale
    bias_grad = bias_sum * scale
    incoming_rows = incoming.reshape(-1, width)
    slot_rows = recv_rows[0].reshape(-1)
    touched = touched_rows[0]
    row_range = jnp.arange(shard_rows, dtype=jnp.int32)
    marks = jnp.any(row_range[:, None] == touched[None, :], axis=1)

    def row_block(row_ids):
        select = (row_ids[:, None] == slot_rows[None, :]).astype(jnp.bfloat16)
        return jnp.dot(select, incoming_rows, preferred_element_type=jnp.float32)

    local_sums = blocked(shard_rows, row_block)
    row_grads = lax.psum(local_sums.astype(jnp.bfloat16), "rep").astype(jnp.float32)
    upd_table, upd_accum = adagrad_rows(emb_table, row_accum, row_grads)
    new_table = jnp.where(marks[:, None], upd_table, emb_table)
    new_accum = jnp.where(marks, upd_accum, row_accum)
    return (weight_grad, bias_grad, dense_grad, new_table, new_accum)


def solution(mesh):
    in_specs = (
        P(("rep", "shard"), None),
        P(("rep", "shard"), None),
        P(),
        P(),
        P("shard", None),
        P("shard"),
        P(("rep", "shard"), None, None),
        P(("rep", "shard"), None),
        P(("rep", "shard"), None, None),
        P("shard", None),
    )
    out_specs = (P(), P(), P(("rep", "shard"), None), P("shard", None), P("shard"))
    return jax.shard_map(
        per_device, mesh=mesh, in_specs=in_specs, out_specs=out_specs, check_vma=False
    )
```

profile of v0, /device:TPU:0, one launch (start us, length us, event | category | flops | bytes accessed | tf_op | source)
XLA Modules:
  0.0 358.1 jit_solution(6436038658471441879)
XLA Ops:
  17.8 102.1 %while.22 = (s32[]{:T(128)}, bf16[16,512,128]{2,1,0:T(8,128)(2,1)}, s32[16,512]{1,0:T(8,128)S(1)}, s32[8192]{0:T(1024)S(1)}, bf16[3584,128]{1,0:T(8,128)(2,1)}, /*index=5*/s32[]{:T(128)}) while((s32[]{:T(128)}, bf16[16,512,128]{2,1,0:T(8,128)(2,1)}, s32[16,512]{1,0:T(8,128)S(1)}, s32[8192]{0:T(1024)S(1)}, ...), condition=%wide.region_5.6_spmd.clone, body=%wide.region_4.5_spmd.clone.sunk | while | flops 471665152 | bytes 1067093 | solution.py:20
  21.0 3.2 fusion.45
  27.4 3.2 fusion.45
  33.8 3.2 fusion.45
  40.1 3.2 fusion.45
  46.5 3.2 fusion.45
  52.9 3.2 fusion.45
  59.3 3.2 fusion.45
  65.7 3.2 fusion.45
  72.1 3.2 fusion.45
  78.4 3.2 fusion.45
  84.8 3.2 fusion.45
  104.0 3.2 fusion.45
  110.4 3.2 fusion.45
  120.0 8.6 %all-to-all-start = ((bf16[32,256,128]{2,1,0:T(8,128)(2,1)}), bf16[32,256,128]{2,1,0:T(8,128)(2,1)}, u32[]{:S(2)}, u32[]{:S(2)}) async-start(bf16[32,256,128]{2,1,0:T(8,128)(2,1)} %bitcast.47), calls=%async_computation | async-start | bytes 4194304 | tf_op jit(solution)/shard_map/all_to_all | solution.py:65
  128.6 4.5 %convolution_bitcast_fusion = f32[1024,1024]{0,1:T(8,128)} fusion(bf16[512,1024]{1,0:T(8,128)(2,1)S(1)} %copy-done.1, bf16[512,1024]{1,0:T(8,128)(2,1)} %param.15), kind=kOutput, calls=%fused_computation.24 | convolution fusion | flops 1075838976 | bytes 6291456 | tf_op jit(solution)/shard_map/dot_general | solution.py:43
  134.8 79.4 %psum.22 = f32[1024]{0:T(1024)S(1)} all-reduce(f32[1024]{0:T(1024)S(1)} %convert_reduce_fusion), channel_id=1, replica_groups=mesh['rep'=4,'shard'=32] {'rep','shard'}, use_global_device_ids=true, to_apply=%region_2.3 | all-reduce | flops 1024 | bytes 8192 | tf_op jit(solution)/shard_map/psum | solution.py:66
  214.2 37.5 %while.21 = (s32[]{:T(128)}, bf16[8,512,128]{2,1,0:T(8,128)(2,1)}, s32[8,512]{1,0:T(8,128)S(1)}, s32[1,32,256]{2,1,0:T(8,128)S(1)}, bf16[8192,128]{1,0:T(8,128)(2,1)}, /*index=5*/s32[]{:T(128)}) while((s32[]{:T(128)}, bf16[8,512,128]{2,1,0:T(8,128)(2,1)}, s32[8,512]{1,0:T(8,128)S(1)}, s32[1,32,256]{2,1,0:T(8,128)S(1)}, ...), condition=%wide.region_7.8_spmd, body=%wide.region_6.7_spmd.sunk | while | flops 1077936128 | bytes 2463829 | solution.py:20
  214.3 4.6 %fusion.43 = bf16[8,512,128]{2,1,0:T(8,128)(2,1)} fusion(bf16[8,512,128]{2,1,0:T(8,128)(2,1)} %get-tuple-element.202, s32[]{:T(128)S(6)} %copy.33, bf16[8192,128]{1,0:T(8,128)(2,1)} %get-tuple-element.211, s32[8192]{0:T(1024)S(1)} %bitcast.50, s32[512]{0:T(512)S(1)} %bitcast.53), kind=kOutput, calls=%fused_computation.7.clone.1 | convolution fusion | flops 1077936128 | bytes 2394116 | tf_op jit(solution)/shard_map/while/body/eval_jaxpr/dot_general | solution.py:77
  219.0 4.6 %fusion.43 = bf16[8,512,128]{2,1,0:T(8,128)(2,1)} fusion(bf16[8,512,128]{2,1,0:T(8,128)(2,1)} %get-tuple-element.202, s32[]{:T(128)S(6)} %copy.33, bf16[8192,128]{1,0:T(8,128)(2,1)} %get-tuple-element.211, s32[8192]{0:T(1024)S(1)} %bitcast.50, s32[512]{0:T(512)S(1)} %bitcast.53), kind=kOutput, calls=%fused_computation.7.clone.1 | convolution fusion | flops 1077936128 | bytes 2394116 | tf_op jit(solution)/shard_map/while/body/eval_jaxpr/dot_general | solution.py:77
  223.6 4.6 %fusion.43 = bf16[8,512,128]{2,1,0:T(8,128)(2,1)} fusion(bf16[8,512,128]{2,1,0:T(8,128)(2,1)} %get-tuple-element.202, s32[]{:T(128)S(6)} %copy.33, bf16[8192,128]{1,0:T(8,128)(2,1)} %get-tuple-element.211, s32[8192]{0:T(1024)S(1)} %bitcast.50, s32[512]{0:T(512)S(1)} %bitcast.53), kind=kOutput, calls=%fused_computation.7.clone.1 | convolution fusion | flops 1077936128 | bytes 2394116 | tf_op jit(solution)/shard_map/while/body/eval_jaxpr/dot_general | solution.py:77
  228.3 4.6 %fusion.43 = bf16[8,512,128]{2,1,0:T(8,128)(2,1)} fusion(bf16[8,512,128]{2,1,0:T(8,128)(2,1)} %get-tuple-element.202, s32[]{:T(128)S(6)} %copy.33, bf16[8192,128]{1,0:T(8,128)(2,1)} %get-tuple-element.211, s32[8192]{0:T(1024)S(1)} %bitcast.50, s32[512]{0:T(512)S(1)} %bitcast.53), kind=kOutput, calls=%fused_computation.7.clone.1 | convolution fusion | flops 1077936128 | bytes 2394116 | tf_op jit(solution)/shard_map/while/body/eval_jaxpr/dot_general | solution.py:77
  233.0 4.6 %fusion.43 = bf16[8,512,128]{2,1,0:T(8,128)(2,1)} fusion(bf16[8,512,128]{2,1,0:T(8,128)(2,1)} %get-tuple-element.202, s32[]{:T(128)S(6)} %copy.33, bf16[8192,128]{1,0:T(8,128)(2,1)} %get-tuple-element.211, s32[8192]{0:T(1024)S(1)} %bitcast.50, s32[512]{0:T(512)S(1)} %bitcast.53), kind=kOutput, calls=%fused_computation.7.clone.1 | convolution fusion | flops 1077936128 | bytes 2394116 | tf_op jit(solution)/shard_map/while/body/eval_jaxpr/dot_general | solution.py:77
  237.7 4.6 %fusion.43 = bf16[8,512,128]{2,1,0:T(8,128)(2,1)} fusion(bf16[8,512,128]{2,1,0:T(8,128)(2,1)} %get-tuple-element.202, s32[]{:T(128)S(6)} %copy.33, bf16[8192,128]{1,0:T(8,128)(2,1)} %get-tuple-element.211, s32[8192]{0:T(1024)S(1)} %bitcast.50, s32[512]{0:T(512)S(1)} %bitcast.53), kind=kOutput, calls=%fused_computation.7.clone.1 | convolution fusion | flops 1077936128 | bytes 2394116 | tf_op jit(solution)/shard_map/while/body/eval_jaxpr/dot_general | solution.py:77
  242.3 4.6 %fusion.43 = bf16[8,512,128]{2,1,0:T(8,128)(2,1)} fusion(bf16[8,512,128]{2,1,0:T(8,128)(2,1)} %get-tuple-element.202, s32[]{:T(128)S(6)} %copy.33, bf16[8192,128]{1,0:T(8,128)(2,1)} %get-tuple-element.211, s32[8192]{0:T(1024)S(1)} %bitcast.50, s32[512]{0:T(512)S(1)} %bitcast.53), kind=kOutput, calls=%fused_computation.7.clone.1 | convolution fusion | flops 1077936128 | bytes 2394116 | tf_op jit(solution)/shard_map/while/body/eval_jaxpr/dot_general | solution.py:77
  247.0 4.7 %fusion.43 = bf16[8,512,128]{2,1,0:T(8,128)(2,1)} fusion(bf16[8,512,128]{2,1,0:T(8,128)(2,1)} %get-tuple-element.202, s32[]{:T(128)S(6)} %copy.33, bf16[8192,128]{1,0:T(8,128)(2,1)} %get-tuple-element.211, s32[8192]{0:T(1024)S(1)} %bitcast.50, s32[512]{0:T(512)S(1)} %bitcast.53), kind=kOutput, calls=%fused_computation.7.clone.1 | convolution fusion | flops 1077936128 | bytes 2394116 | tf_op jit(solution)/shard_map/while/body/eval_jaxpr/dot_general | solution.py:77
  253.9 4.1 %fusion.17 = pred[4096]{0:T(1024)(128)(4,1)S(1)} fusion(s32[2048]{0:T(1024)S(1)} %bitcast.56), kind=kLoop, calls=%fused_computation.18 | loop fusion | flops 16773120 | bytes 12288 | tf_op jit(solution)/shard_map/reduce_or | solution.py:73
  258.0 39.7 %all-reduce.3.cloned.1.call-done = f32[1024,1024]{0,1:T(8,128)} async-done(((f32[1024,1024]{0,1:T(8,128)}), f32[1024,1024]{0,1:T(8,128)}) %all-reduce.3.cloned.1.call-update) | async-done | bytes 4194320 | tf_op jit(solution)/shard_map/psum | solution.py:66
  297.7 5.0 %broadcast_multiply_fusion = f32[1024,1024]{0,1:T(8,128)} fusion(f32[1024,1024]{0,1:T(8,128)} %all-reduce.3.cloned.1.call-done), kind=kLoop, calls=%fused_computation.33 | loop fusion | flops 1048576 | bytes 8388608 | tf_op jit(solution)/shard_map/mul | solution.py:67
  302.7 5.4 %copy.17 = f32[1024,1024]{1,0:T(8,128)} copy(f32[1024,1024]{0,1:T(8,128)} %broadcast_multiply_fusion) | data formatting | bytes 8388608
  308.0 36.2 %all-reduce.5.cloned.1.call-done = bf16[4096,128]{1,0:T(8,128)(2,1)} async-done(((bf16[4096,128]{1,0:T(8,128)(2,1)}), bf16[4096,128]{1,0:T(8,128)(2,1)}) %all-reduce.5.cloned.1.call-update) | async-done | bytes 1048592 | tf_op jit(solution)/shard_map/psum | solution.py:80
  346.8 4.5 %fusion.20 = f32[4096,128]{1,0:T(8,128)} fusion(f32[4096,128]{1,0:T(8,128)} %param.18, bf16[4096,128]{1,0:T(8,128)(2,1)} %all-reduce.5.cloned.1.call-done, f32[4096]{0:T(1024)S(1)} %get-tuple-element.114, pred[4096]{0:T(1024)(128)(4,1)S(1)} %fusion.17), kind=kLoop, calls=%fused_computation.27 | loop fusion | flops 3145728 | bytes 5263360 | tf_op jit(solution)/shard_map/jit(_where)/select_n | solution.py:82
  (105 shorter events, 77.2 us)
Async XLA Ops:
  7.2 1.7 copy-start
  8.9 2.7 copy-start.1
  8.9 2.7 copy-start.2
  8.9 2.7 copy-start.7
  13.1 1.0 copy-start.3
  120.0 94.2 %all-to-all-start = ((bf16[32,256,128]{2,1,0:T(8,128)(2,1)}), bf16[32,256,128]{2,1,0:T(8,128)(2,1)}, u32[]{:S(2)}, u32[]{:S(2)}) async-start(bf16[32,256,128]{2,1,0:T(8,128)(2,1)} %bitcast.47), calls=%async_computation | async-start | bytes 4194304 | tf_op jit(solution)/shard_map/all_to_all | solution.py:65
  128.5 169.1 %all-reduce.3.cloned.1.call-start = ((), (), s32[]{:S(2)}) async-start(), calls=%async_computation.1 | async-start | bytes 8388608 | tf_op jit(solution)/shard_map/psum | solution.py:66
  133.2 81.0 %copy-start.4 = (s32[1,32,256]{2,1,0:T(8,128)S(1)}, s32[1,32,256]{2,1,0:T(8,128)}, u32[]{:S(2)}) copy-start(s32[1,32,256]{2,1,0:T(8,128)} %param.22) | copy-start | bytes 98308
  133.2 211.1 %all-reduce.5.cloned.1.call-start = ((), (), s32[]{:S(2)}) async-start(), calls=%async_computation.2 | async-start | bytes 2097152 | tf_op jit(solution)/shard_map/psum | solution.py:80
  214.2 39.7 %copy-start.6 = (s32[1,2048]{1,0:T(1,128)S(1)}, s32[1,2048]{1,0:T(1,128)}, u32[]{:S(2)}) copy-start(s32[1,2048]{1,0:T(1,128)} %param.23) | copy-start | bytes 24580
  302.7 43.5 %copy-start.5 = (f32[4096]{0:T(1024)S(1)}, f32[4096]{0:T(1024)}, u32[]{:S(2)}) copy-start(f32[4096]{0:T(1024)} %param.19) | copy-start | bytes 49156
Sparse Core Ops, SparseCore 0:
  134.8 162.7 all-reduce.2
  300.0 44.2 all-reduce.4
where the time goes:
time: 360 us; the launch traced here: 358 us
  matrix products  97.1 us (27%)
  blocking collectives  79.4 us (22%)
  waiting for transfers between devices  76 us (21%)
  local copies, waits for them, and re-layouts  63 us (18%)
  other arithmetic  19.4 us (5%)
  between operations  14.2 us (4%)
  starting transfers between devices  8.65 us (2%)
    psum x1, blocking collectives, per_device(): weight_sum, bias_sum = lax.psum((weight_part, bias_part), ('rep', 'shard'))  79.4 us
    dot_general x16, matrix products, pick_bags(): jnp.dot(select, pooled, preferred_element_type=jnp.float32)  51.3 us
    gather x16, local copies, waits for them, and re-layouts, pick_bags(): flat_bags[positions][:, None] == bag_range[None, :]  50.3 us
    psum x1, waiting for transfers between devices, per_device(): weight_sum, bias_sum = lax.psum((weight_part, bias_part), ('rep', 'shard'))  39.7 us
    dot_general x8, matrix products, row_block(): return jnp.dot(select, incoming_rows, preferred_element_type=jnp.float32)  37.1 us
    psum x1, waiting for transfers between devices, per_device(): lax.psum(local_sums.astype(jnp.bfloat16), 'rep').astype(jnp.float32)  36.2 us
    all_to_all x1, starting transfers between devices, per_device(): lax.all_to_all(outgoing, 'shard', split_axis=0, concat_axis=0, tiled=True)  8.57 us
  transfers between devices with their start and end apart: 3, of which 2 were waited for; matrix products, arithmetic and copies ran while one was open for 17% of the time, Pallas kernels for 0%

commit v1 on v0

--- a/solution.py
+++ b/solution.py
@@ -6,6 +6,12 @@
 
 learn_rate = 0.5
 keep_rate = 0.9
+
+
+def gather_and_add(value, mesh_axis):
+    pieces = lax.all_gather(value, mesh_axis, axis=0, tiled=False)
+    result = pieces.sum(axis=0)
+    return result
 
 
 def adagrad_rows(table_rows, accum_rows, grads):
@@ -77,7 +83,7 @@
         return jnp.dot(select, incoming_rows, preferred_element_type=jnp.float32)
 
     local_sums = blocked(shard_rows, row_block)
-    row_grads = lax.psum(local_sums.astype(jnp.bfloat16), "rep").astype(jnp.float32)
+    row_grads = gather_and_add(local_sums.astype(jnp.bfloat16), "rep").astype(jnp.float32)
     upd_table, upd_accum = adagrad_rows(emb_table, row_accum, row_grads)
     new_table = jnp.where(marks[:, None], upd_table, emb_table)
     new_accum = jnp.where(marks, upd_accum, row_accum)

time: 360 us -> 347 us (0.964)
  blocking collectives: 79.4 us -> 68 us
  waiting for transfers between devices: 76 us -> 68.7 us
    psum x1 -> x0, waiting for transfers between devices: 36.2 us -> none  [per_device(): lax.psum(local_sums.astype(jnp.bfloat16), 'rep').astype(jnp.float32)]
    all_to_all x1, waiting for transfers between devices: 0.01 us -> 25.9 us  [per_device(): lax.all_to_all(outgoing, 'shard', split_axis=0, concat_axis=0, tiled=True)]
    psum x1, blocking collectives: 79.4 us -> 68 us  [per_device(): weight_sum, bias_sum = lax.psum((weight_part, bias_part), ('rep', 'shard'))]
where the time goes in v1:
time: 347 us; the launch traced here: 345 us
  matrix products  97.3 us (28%)
  waiting for transfers between devices  68.7 us (20%)
  blocking collectives  68 us (20%)
  local copies, waits for them, and re-layouts  63 us (18%)
  other arithmetic  22.9 us (7%)
  between operations  15.6 us (4%)
  starting transfers between devices  8.66 us (2%)
    psum x1, blocking collectives, per_device(): weight_sum, bias_sum = lax.psum((weight_part, bias_part), ('rep', 'shard'))  68 us
    dot_general x16, matrix products, pick_bags(): jnp.dot(select, pooled, preferred_element_type=jnp.float32)  51.3 us
    gather x16, local copies, waits for them, and re-layouts, pick_bags(): flat_bags[positions][:, None] == bag_range[None, :]  50.3 us
    psum x1, waiting for transfers between devices, per_device(): weight_sum, bias_sum = lax.psum((weight_part, bias_part), ('rep', 'shard'))  42.8 us
    dot_general x8, matrix products, row_block(): return jnp.dot(select, incoming_rows, preferred_element_type=jnp.float32)  37.2 us
    all_to_all x1, waiting for transfers between devices, per_device(): lax.all_to_all(outgoing, 'shard', split_axis=0, concat_axis=0, tiled=True)  25.9 us
    all_to_all x1, starting transfers between devices, per_device(): lax.all_to_all(outgoing, 'shard', split_axis=0, concat_axis=0, tiled=True)  8.58 us
    unnamed x18, local copies, waits for them, and re-layouts  7.2 us
  transfers between devices with their start and end apart: 3, of which 2 were waited for; matrix products, arithmetic and copies ran while one was open for 17% of the time, Pallas kernels for 0%

profile of v1, /device:TPU:0, one launch (start us, length us, event | category | flops | bytes accessed | tf_op | source)
XLA Modules:
  0.0 344.6 jit_solution(6260563884428290327)
XLA Ops:
  18.7 102.1 %while.22 = (s32[]{:T(128)}, bf16[16,512,128]{2,1,0:T(8,128)(2,1)}, s32[16,512]{1,0:T(8,128)S(1)}, s32[8192]{0:T(1024)S(1)}, bf16[3584,128]{1,0:T(8,128)(2,1)}, /*index=5*/s32[]{:T(128)}) while((s32[]{:T(128)}, bf16[16,512,128]{2,1,0:T(8,128)(2,1)}, s32[16,512]{1,0:T(8,128)S(1)}, s32[8192]{0:T(1024)S(1)}, ...), condition=%wide.region_5.6_spmd.clone, body=%wide.region_4.5_spmd.clone.sunk | while | flops 471665152 | bytes 1067093 | solution.py:26
  21.9 3.2 fusion.45
  41.0 3.2 fusion.45
  47.4 3.2 fusion.45
  53.8 3.2 fusion.45
  60.2 3.2 fusion.45
  66.6 3.2 fusion.45
  73.0 3.2 fusion.45
  79.3 3.2 fusion.45
  98.5 3.2 fusion.45
  104.9 3.2 fusion.45
  111.3 3.2 fusion.45
  117.6 3.2 fusion.45
  120.9 8.6 %all-to-all-start = ((bf16[32,256,128]{2,1,0:T(8,128)(2,1)}), bf16[32,256,128]{2,1,0:T(8,128)(2,1)}, u32[]{:S(2)}, u32[]{:S(2)}) async-start(bf16[32,256,128]{2,1,0:T(8,128)(2,1)} %bitcast.47), calls=%async_computation | async-start | bytes 4194304 | tf_op jit(solution)/shard_map/all_to_all | solution.py:71
  129.5 4.5 %convolution_bitcast_fusion = f32[1024,1024]{0,1:T(8,128)} fusion(bf16[512,1024]{1,0:T(8,128)(2,1)S(1)} %copy-done.1, bf16[512,1024]{1,0:T(8,128)(2,1)} %param.15), kind=kOutput, calls=%fused_computation.24 | convolution fusion | flops 1075838976 | bytes 6291456 | tf_op jit(solution)/shard_map/dot_general | solution.py:49
  134.1 25.9 %all-to-all-done = bf16[32,256,128]{2,1,0:T(8,128)(2,1)} async-done(((bf16[32,256,128]{2,1,0:T(8,128)(2,1)}), bf16[32,256,128]{2,1,0:T(8,128)(2,1)}, u32[]{:S(2)}, u32[]{:S(2)}) %all-to-all-start) | async-done | bytes 2097184 | tf_op jit(solution)/shard_map/all_to_all | solution.py:71
  160.0 37.6 %while.21 = (s32[]{:T(128)}, bf16[8,512,128]{2,1,0:T(8,128)(2,1)}, s32[8,512]{1,0:T(8,128)S(1)}, s32[1,32,256]{2,1,0:T(8,128)S(1)}, bf16[8192,128]{1,0:T(8,128)(2,1)}, /*index=5*/s32[]{:T(128)}) while((s32[]{:T(128)}, bf16[8,512,128]{2,1,0:T(8,128)(2,1)}, s32[8,512]{1,0:T(8,128)S(1)}, s32[1,32,256]{2,1,0:T(8,128)S(1)}, ...), condition=%wide.region_7.8_spmd, body=%wide.region_6.7_spmd.sunk | while | flops 1077936128 | bytes 2463829 | solution.py:26
  160.0 4.7 %fusion.43 = bf16[8,512,128]{2,1,0:T(8,128)(2,1)} fusion(bf16[8,512,128]{2,1,0:T(8,128)(2,1)} %get-tuple-element.207, s32[]{:T(128)S(6)} %copy.34, bf16[8192,128]{1,0:T(8,128)(2,1)} %get-tuple-element.216, s32[8192]{0:T(1024)S(1)} %bitcast.50, s32[512]{0:T(512)S(1)} %bitcast.53), kind=kOutput, calls=%fused_computation.7.clone.1 | convolution fusion | flops 1077936128 | bytes 2394116 | tf_op jit(solution)/shard_map/while/body/eval_jaxpr/dot_general | solution.py:83
  164.8 4.7 %fusion.43 = bf16[8,512,128]{2,1,0:T(8,128)(2,1)} fusion(bf16[8,512,128]{2,1,0:T(8,128)(2,1)} %get-tuple-element.207, s32[]{:T(128)S(6)} %copy.34, bf16[8192,128]{1,0:T(8,128)(2,1)} %get-tuple-element.216, s32[8192]{0:T(1024)S(1)} %bitcast.50, s32[512]{0:T(512)S(1)} %bitcast.53), kind=kOutput, calls=%fused_computation.7.clone.1 | convolution fusion | flops 1077936128 | bytes 2394116 | tf_op jit(solution)/shard_map/while/body/eval_jaxpr/dot_general | solution.py:83
  169.5 4.6 %fusion.43 = bf16[8,512,128]{2,1,0:T(8,128)(2,1)} fusion(bf16[8,512,128]{2,1,0:T(8,128)(2,1)} %get-tuple-element.207, s32[]{:T(128)S(6)} %copy.34, bf16[8192,128]{1,0:T(8,128)(2,1)} %get-tuple-element.216, s32[8192]{0:T(1024)S(1)} %bitcast.50, s32[512]{0:T(512)S(1)} %bitcast.53), kind=kOutput, calls=%fused_computation.7.clone.1 | convolution fusion | flops 1077936128 | bytes 2394116 | tf_op jit(solution)/shard_map/while/body/eval_jaxpr/dot_general | solution.py:83
  174.2 4.7 %fusion.43 = bf16[8,512,128]{2,1,0:T(8,128)(2,1)} fusion(bf16[8,512,128]{2,1,0:T(8,128)(2,1)} %get-tuple-element.207, s32[]{:T(128)S(6)} %copy.34, bf16[8192,128]{1,0:T(8,128)(2,1)} %get-tuple-element.216, s32[8192]{0:T(1024)S(1)} %bitcast.50, s32[512]{0:T(512)S(1)} %bitcast.53), kind=kOutput, calls=%fused_computation.7.clone.1 | convolution fusion | flops 1077936128 | bytes 2394116 | tf_op jit(solution)/shard_map/while/body/eval_jaxpr/dot_general | solution.py:83
  178.9 4.6 %fusion.43 = bf16[8,512,128]{2,1,0:T(8,128)(2,1)} fusion(bf16[8,512,128]{2,1,0:T(8,128)(2,1)} %get-tuple-element.207, s32[]{:T(128)S(6)} %copy.34, bf16[8192,128]{1,0:T(8,128)(2,1)} %get-tuple-element.216, s32[8192]{0:T(1024)S(1)} %bitcast.50, s32[512]{0:T(512)S(1)} %bitcast.53), kind=kOutput, calls=%fused_computation.7.clone.1 | convolution fusion | flops 1077936128 | bytes 2394116 | tf_op jit(solution)/shard_map/while/body/eval_jaxpr/dot_general | solution.py:83
  183.6 4.6 %fusion.43 = bf16[8,512,128]{2,1,0:T(8,128)(2,1)} fusion(bf16[8,512,128]{2,1,0:T(8,128)(2,1)} %get-tuple-element.207, s32[]{:T(128)S(6)} %copy.34, bf16[8192,128]{1,0:T(8,128)(2,1)} %get-tuple-element.216, s32[8192]{0:T(1024)S(1)} %bitcast.50, s32[512]{0:T(512)S(1)} %bitcast.53), kind=kOutput, calls=%fused_computation.7.clone.1 | convolution fusion | flops 1077936128 | bytes 2394116 | tf_op jit(solution)/shard_map/while/body/eval_jaxpr/dot_general | solution.py:83
  188.3 4.6 %fusion.43 = bf16[8,512,128]{2,1,0:T(8,128)(2,1)} fusion(bf16[8,512,128]{2,1,0:T(8,128)(2,1)} %get-tuple-element.207, s32[]{:T(128)S(6)} %copy.34, bf16[8192,128]{1,0:T(8,128)(2,1)} %get-tuple-element.216, s32[8192]{0:T(1024)S(1)} %bitcast.50, s32[512]{0:T(512)S(1)} %bitcast.53), kind=kOutput, calls=%fused_computation.7.clone.1 | convolution fusion | flops 1077936128 | bytes 2394116 | tf_op jit(solution)/shard_map/while/body/eval_jaxpr/dot_general | solution.py:83
  192.9 4.6 %fusion.43 = bf16[8,512,128]{2,1,0:T(8,128)(2,1)} fusion(bf16[8,512,128]{2,1,0:T(8,128)(2,1)} %get-tuple-element.207, s32[]{:T(128)S(6)} %copy.34, bf16[8192,128]{1,0:T(8,128)(2,1)} %get-tuple-element.216, s32[8192]{0:T(1024)S(1)} %bitcast.50, s32[512]{0:T(512)S(1)} %bitcast.53), kind=kOutput, calls=%fused_computation.7.clone.1 | convolution fusion | flops 1077936128 | bytes 2394116 | tf_op jit(solution)/shard_map/while/body/eval_jaxpr/dot_general | solution.py:83
  200.7 68.0 %psum.15 = f32[1024]{0:T(1024)S(1)} all-reduce(f32[1024]{0:T(1024)S(1)} %convert_reduce_fusion), channel_id=1, replica_groups=mesh['rep'=4,'shard'=32] {'rep','shard'}, use_global_device_ids=true, to_apply=%region_2.3 | all-reduce | flops 1024 | bytes 8192 | tf_op jit(solution)/shard_map/psum | solution.py:72
  269.3 4.1 %fusion.17 = pred[4096]{0:T(1024)(128)(4,1)S(1)} fusion(s32[2048]{0:T(1024)S(1)} %bitcast.56), kind=kLoop, calls=%fused_computation.18 | loop fusion | flops 16773120 | bytes 12288 | tf_op jit(solution)/shard_map/reduce_or | solution.py:79
  273.5 42.8 %all-reduce.2.cloned.1.call-done = f32[1024,1024]{0,1:T(8,128)} async-done(((f32[1024,1024]{0,1:T(8,128)}), f32[1024,1024]{0,1:T(8,128)}) %all-reduce.2.cloned.1.call-update) | async-done | bytes 4194320 | tf_op jit(solution)/shard_map/psum | solution.py:72
  316.3 5.0 %broadcast_multiply_fusion = f32[1024,1024]{0,1:T(8,128)} fusion(f32[1024,1024]{0,1:T(8,128)} %all-reduce.2.cloned.1.call-done), kind=kLoop, calls=%fused_computation.33 | loop fusion | flops 1048576 | bytes 8388608 | tf_op jit(solution)/shard_map/mul | solution.py:73
  321.3 5.3 %copy.18 = f32[1024,1024]{1,0:T(8,128)} copy(f32[1024,1024]{0,1:T(8,128)} %broadcast_multiply_fusion) | data formatting | bytes 8388608
  326.6 3.5 %reduce_sum.31 = bf16[4096,128]{1,0:T(8,128)(2,1)S(1)} reduce(bf16[4,4096,128]{2,1,0:T(8,128)(2,1)} %all-gather.2.cloned.1.call-done, bf16[]{:T(256)} %constant.42.clone.1), dimensions={0}, to_apply=%region_8.9 | reduce | flops 1572864 | bytes 5242882 | tf_op jit(solution)/shard_map/reduce_sum | solution.py:13
  331.4 5.8 %fusion.20 = f32[4096,128]{1,0:T(8,128)} fusion(f32[4096,128]{1,0:T(8,128)} %param.18, bf16[4096,128]{1,0:T(8,128)(2,1)S(1)} %reduce_sum.31, f32[4096]{0:T(1024)S(1)} %get-tuple-element.119, pred[4096]{0:T(1024)(128)(4,1)S(1)} %fusion.17), kind=kLoop, calls=%fused_computation.27 | loop fusion | flops 3145728 | bytes 5263360 | tf_op jit(solution)/shard_map/jit(_where)/select_n | solution.py:88
  (106 shorter events, 79.3 us)
Async XLA Ops:
  8.0 1.7 copy-start
  9.7 2.7 copy-start.1
  9.7 2.7 copy-start.2
  9.7 2.7 copy-start.7
  13.9 1.0 copy-start.3
  120.9 39.1 %all-to-all-start = ((bf16[32,256,128]{2,1,0:T(8,128)(2,1)}), bf16[32,256,128]{2,1,0:T(8,128)(2,1)}, u32[]{:S(2)}, u32[]{:S(2)}) async-start(bf16[32,256,128]{2,1,0:T(8,128)(2,1)} %bitcast.47), calls=%async_computation | async-start | bytes 4194304 | tf_op jit(solution)/shard_map/all_to_all | solution.py:71
  129.4 186.9 %all-reduce.2.cloned.1.call-start = ((), (), s32[]{:S(2)}) async-start(), calls=%async_computation.1 | async-start | bytes 8388608 | tf_op jit(solution)/shard_map/psum | solution.py:72
  134.0 26.0 %copy-start.4 = (s32[1,32,256]{2,1,0:T(8,128)S(1)}, s32[1,32,256]{2,1,0:T(8,128)}, u32[]{:S(2)}) copy-start(s32[1,32,256]{2,1,0:T(8,128)} %param.22) | copy-start | bytes 98308
  134.1 192.6 %all-gather.2.cloned.1.call-start = ((), (), s32[]{:S(2)}) async-start(), calls=%async_computation.2 | async-start | bytes 5242880 | tf_op jit(solution)/shard_map/all_gather | solution.py:12
  197.6 71.8 %copy-start.6 = (s32[1,2048]{1,0:T(1,128)S(1)}, s32[1,2048]{1,0:T(1,128)}, u32[]{:S(2)}) copy-start(s32[1,2048]{1,0:T(1,128)} %param.23) | copy-start | bytes 24580
  326.6 4.1 %copy-start.5 = (f32[4096]{0:T(1024)S(1)}, f32[4096]{0:T(1024)}, u32[]{:S(2)}) copy-start(f32[4096]{0:T(1024)} %param.19) | copy-start | bytes 49156
Sparse Core Ops, SparseCore 0:
  135.8 180.4 all-reduce.1
Sparse Core Ops, SparseCore 1:
  197.7 48.4 all-gather.1
